TPU v7x, 32 devices: a whole 2x2x4 slice. The times are simulated.
32 devices in a mesh: dp: 4 (over y, x), expert: 8 (over z, core).
Axes of the slice: x: 2, y: 2, z: 4, core: 2. Of those that a mesh axis runs over, the one named last changes fastest.
Arguments:
- hidden: bfloat16 [32, 2048], P(('dp', 'expert')), may hold values from -6 to 6
- attn_gain: float32 [2048], replicated, may hold values from 0.25 to 1.75
- query_weight: bfloat16 [3072, 2048], P('expert'), may hold values from -0.125 to 0.125
- latent_down: bfloat16 [2048, 576], replicated, may hold values from -0.125 to 0.125
- latent_up: bfloat16 [512, 4096], P(None, 'expert'), may hold values from -0.25 to 0.25
- out_weight: bfloat16 [2048, 2048], P('expert'), may hold values from -0.125 to 0.125
- latent_pool: bfloat16 [128, 32, 576], P('dp'), may hold values from -1000 to 1000
- page_table: int32 [32, 16], replicated, may hold values from -1 to 127, as said below
- page_counts: int32 [32], replicated, may hold values from 1 to 16, as said below
- ffn_gain: float32 [2048], replicated, may hold values from 0.25 to 1.75
- expert_ids: int32 [32, 6], replicated, may hold values from 0 to 23, all different within a row; in each aligned block of 32 rows (0 to 31, 32 to 63, ...) at most 16 rows name the same one
- expert_gates: float32 [32, 6], replicated, may hold values from 0.05 to 0.6
- old_place: int32 [8, 4], replicated, may hold values from 0 to 23, as said below
- new_place: int32 [8, 4], replicated, may hold values from 0 to 23, as said below
- expert_gate_up: bfloat16 [32, 2, 1408, 2048], P('expert', None, None, 'dp'), as said below
- expert_down: bfloat16 [32, 1408, 2048], P('expert', None, 'dp'), as said below
- shared_gate_up: bfloat16 [2, 2816, 2048], P(None, None, 'dp'), may hold values from -0.125 to 0.125
- shared_down: bfloat16 [2816, 2048], P(None, 'dp'), may hold values from -0.109375 to 0.109375
Outputs:
- layer_out: bfloat16 [32, 2048], P(('dp', 'expert'))
- moved_gate_up: bfloat16 [32, 2, 1408, 2048], P('expert', None, None, 'dp')
- moved_down: bfloat16 [32, 1408, 2048], P('expert', None, 'dp')
Inputs may be any that keep to these rules, and one draw needn't show every extreme that they name: `page_counts`: each request's count of cached pages; exactly one request has 16. `page_table`: row t names page_counts[t] pages of the pool, no page named twice in the table; its other entries are -1. Page p lies on dp index p // 32. `expert_ids`: no expert is named by more than 16 tokens in all; some expert by exactly 16. `old_place`: row i holds the experts of the slots on expert index i, slot s of row i being global slot i * 4 + s; every expert is held by one slot or more. `new_place`: equal to old_place except in exactly one slot of each row, which names another expert. `expert_gate_up`: slots that hold the same expert under old_place hold equal weights. `expert_down`: slots that hold the same expert under old_place hold equal weights.
All inputs are finite; a program needn't handle non-finite values.
Results may differ from a plain program's by a relative error of at most 0.02.
Values may be sent and summed in bfloat16 or wider, within the bound.
No kernel may reach another device: no remote copies, remote signals or barrier semaphores. Data moves between devices by JAX's collectives and lax.ppermute only.
A program may use at most 128 MiB of HBM per device.

v0:
```python
import math

import jax
import jax.numpy as jnp
from jax import lax
from jax.sharding import PartitionSpec as P

NOPE = 128
ROPE = 64
VHEAD = 128
LATENT = 512
EXP_DEV = 3
PAGE = 32


EPSILON = 1e-06
ROPE_BASE = 50000.0
MASKED_SCORE = -1e30
HIGHEST = lax.Precision.HIGHEST


def combined_all(part, axis, combine):
    gathered = jax.tree.map(lambda a: lax.all_gather(a, axis), part)

    def take(source):
        return jax.tree.map(lambda a: lax.dynamic_index_in_dim(a, source, 0, False), gathered)

    return lax.fori_loop(
        1, lax.axis_size(axis), lambda source, state: combine(state, take(source)), take(0)
    )


def rms_plain(values):
    mean_square = jnp.mean(values * values, axis=-1, keepdims=True)
    return values * lax.rsqrt(mean_square + EPSILON)


def rms_norm(values, norm_gain):
    return rms_plain(values) * norm_gain


def rotary(values, position):
    half_width = values.shape[-1] // 2
    exponent = jnp.arange(half_width).astype(jnp.float32) * (2.0 / values.shape[-1])
    frequency = jnp.exp(-exponent * math.log(ROPE_BASE))
    angles = position[..., None] * frequency
    cosine = jnp.cos(angles)
    sine_part = jnp.sin(angles)
    first_half = values[..., :half_width]
    second = values[..., half_width:]
    return jnp.concatenate(
        [first_half * cosine - second * sine_part, second * cosine + first_half * sine_part],
        axis=-1,
    )


def combine_parts(earlier, later):
    highest = jnp.maximum(earlier[0], later[0])
    weight_early = jnp.exp(earlier[0] - highest)
    weight_late = jnp.exp(later[0] - highest)
    return (
        highest,
        earlier[1] * weight_early + later[1] * weight_late,
        earlier[2] * weight_early[..., None] + later[2] * weight_late[..., None],
    )


def local(
    hidden,
    attn_gain,
    query_weight,
    latent_down,
    latent_up,
    out_weight,
    latent_pool,
    page_table,
    page_counts,
    ffn_gain,
    expert_ids,
    expert_gates,
    old_place,
    new_place,
    expert_gate_up,
    expert_down,
    shared_gate_up,
    shared_down,
):
    dp_count = lax.axis_size("dp")
    ex_count = lax.axis_size("expert")
    dp_index = lax.axis_index("dp")
    ex_index = lax.axis_index("expert")
    req_local = hidden.shape[0]
    group_rows = req_local * ex_count
    requests = page_counts.shape[0]
    head_local = query_weight.shape[0] // (NOPE + ROPE)
    score_scale = (NOPE + ROPE) ** (-0.5)
    group_start = dp_index * group_rows
    everyone = lax.all_gather(hidden, ("dp", "expert"), axis=0, tiled=True)
    normed = rms_norm(everyone.astype(jnp.float32), attn_gain).astype(jnp.bfloat16)
    queries = jnp.einsum(
        "td,qd->tq", normed, query_weight, preferred_element_type=jnp.float32
    ).reshape(requests, head_local, NOPE + ROPE)
    position = (page_counts * PAGE).astype(jnp.float32)
    query_rope = rotary(queries[..., NOPE:], position[:, None]).astype(jnp.bfloat16)
    up_table = latent_up.reshape(LATENT, head_local, NOPE + VHEAD)
    query_latent = jnp.einsum(
        "thn,lhn->thl",
        queries[..., :NOPE],
        up_table[..., :NOPE].astype(jnp.float32),
        precision=HIGHEST,
    ).astype(jnp.bfloat16)
    pages_local = latent_pool.shape[0]
    pool_total = pages_local * dp_count
    flat_pages = page_table.reshape(-1)
    flat_owner = jnp.repeat(jnp.arange(requests, dtype=jnp.int32), page_table.shape[1])
    target = jnp.where(flat_pages >= 0, flat_pages, pool_total)
    owner_all = jnp.full((pool_total,), -1, jnp.int32).at[target].set(flat_owner, mode="drop")
    page_owner = lax.dynamic_slice_in_dim(owner_all, dp_index * pages_local, pages_local)
    page_used = page_owner >= 0
    owner_safe = jnp.maximum(page_owner, 0)
    page_latent = latent_pool[..., :LATENT]
    page_rope = latent_pool[..., LATENT:]
    scores = jnp.einsum(
        "phl,pkl->phk", query_latent[owner_safe], page_latent, preferred_element_type=jnp.float32
    )
    scores = (
        scores
        + jnp.einsum(
            "phr,pkr->phk", query_rope[owner_safe], page_rope, preferred_element_type=jnp.float32
        )
    ) * score_scale
    raw_max = jnp.max(scores, axis=2)
    weights = jnp.exp(scores - raw_max[..., None])
    page_total = jnp.sum(weights, axis=2)
    page_mix = jnp.einsum(
        "phk,pkl->phl",
        weights.astype(jnp.bfloat16),
        page_latent,
        preferred_element_type=jnp.float32,
    )
    page_max = jnp.where(page_used[:, None], raw_max, MASKED_SCORE)
    member = page_owner[None, :] == jnp.arange(requests, dtype=jnp.int32)[:, None]
    req_max = jnp.max(jnp.where(member[:, :, None], page_max[None], MASKED_SCORE), axis=1)
    rescale = jnp.where(page_used[:, None], jnp.exp(page_max - req_max[owner_safe]), 0.0)
    member_float = member.astype(jnp.float32)
    req_total = jnp.dot(member_float, page_total * rescale, precision=HIGHEST)
    req_mix = jnp.einsum(
        "rp,phl->rhl", member_float, page_mix * rescale[..., None], precision=HIGHEST
    )
    merged = combined_all((req_max, req_total, req_mix), "dp", combine_parts)
    part_max = lax.dynamic_slice_in_dim(merged[0], group_start, group_rows, 0)
    part_total = lax.dynamic_slice_in_dim(merged[1], group_start, group_rows, 0)
    part_mix = lax.dynamic_slice_in_dim(merged[2], group_start, group_rows, 0)
    own_normed = lax.dynamic_slice_in_dim(normed, group_start, group_rows, 0)
    own_position = lax.dynamic_slice_in_dim(position, group_start, group_rows, 0)
    fresh_latent = jnp.dot(own_normed, latent_down, preferred_element_type=jnp.float32)
    new_latent = rms_plain(fresh_latent[:, :LATENT]).astype(jnp.bfloat16)
    new_rope = rotary(fresh_latent[:, LATENT:], own_position).astype(jnp.bfloat16)
    own_query = lax.dynamic_slice_in_dim(query_latent, group_start, group_rows, 0)
    own_rope_query = lax.dynamic_slice_in_dim(query_rope, group_start, group_rows, 0)
    own_score = jnp.einsum("thl,tl->th", own_query, new_latent, preferred_element_type=jnp.float32)
    own_score = (
        own_score
        + jnp.einsum("thr,tr->th", own_rope_query, new_rope, preferred_element_type=jnp.float32)
    ) * score_scale
    highest = jnp.maximum(part_max, own_score)
    kept_part = jnp.exp(part_max - highest)
    own_weight = jnp.exp(own_score - highest)
    denominator = part_total * kept_part + own_weight
    numerator = (
        part_mix * kept_part[..., None]
        + own_weight[..., None] * new_latent.astype(jnp.float32)[:, None, :]
    )
    attended = (numerator / denominator[..., None]).astype(jnp.bfloat16)
    heads_out = jnp.einsum(
        "thl,lhv->thv", attended, up_table[..., NOPE:], preferred_element_type=jnp.float32
    )
    heads_out = heads_out.astype(jnp.bfloat16).reshape(group_rows, head_local * VHEAD)
    partial_value = jnp.dot(heads_out, out_weight, preferred_element_type=jnp.float32)
    attn_out = lax.psum_scatter(partial_value, "expert", scatter_dimension=0, tiled=True)
    residual = hidden.astype(jnp.float32) + attn_out
    normed_ffn = rms_norm(residual, ffn_gain).astype(jnp.bfloat16)
    slots_local = expert_gate_up.shape[0]
    ff_width = expert_gate_up.shape[2]
    col_width = expert_gate_up.shape[3]
    every_row = lax.all_gather(normed_ffn, ("dp", "expert"), axis=0, tiled=True)
    my_columns = lax.dynamic_slice_in_dim(every_row, dp_index * col_width, col_width, 1)
    by_group = my_columns.reshape(dp_count, ex_count, req_local, col_width).transpose(1, 0, 2, 3)
    ffn_rows = by_group.reshape(requests, col_width)
    column_rows = lax.dynamic_index_in_dim(by_group, ex_index, 0, keepdims=False).reshape(
        dp_count * req_local, col_width
    )
    top_count = expert_ids.shape[1]
    experts_count = EXP_DEV * ex_count
    ids_order = (
        expert_ids.reshape(dp_count, ex_count, req_local, top_count)
        .transpose(1, 0, 2, 3)
        .reshape(requests, top_count)
    )
    gates_order = (
        expert_gates.reshape(dp_count, ex_count, req_local, top_count)
        .transpose(1, 0, 2, 3)
        .reshape(requests, top_count)
    )
    old_flat = old_place.reshape(-1)
    holds_map = old_flat[None, :] == jnp.arange(experts_count, dtype=jnp.int32)[:, None]
    holder = jnp.argmax(holds_map, axis=1)
    slot_of = holder[ids_order.reshape(-1)]
    capacity = 2 * requests * top_count // experts_count
    local_slot = slot_of - ex_index * slots_local
    slot_hot = local_slot[:, None] == jnp.arange(slots_local, dtype=jnp.int32)[None, :]
    slot_rank = jnp.cumsum(slot_hot.astype(jnp.int32), axis=0) - 1
    position_in = jnp.where(slot_hot, slot_rank, capacity)
    route_hot = (
        position_in[:, :, None] == jnp.arange(capacity, dtype=jnp.int32)[None, None, :]
    ).astype(jnp.float32)
    route_hot = route_hot.reshape(requests, top_count, slots_local, capacity)
    dispatch = jnp.sum(route_hot, axis=1).astype(jnp.bfloat16)
    combine = jnp.sum(route_hot * gates_order[:, :, None, None], axis=1)
    slot_inputs = jnp.einsum(
        "tsc,td->scd", dispatch, ffn_rows, preferred_element_type=jnp.float32
    ).astype(jnp.bfloat16)
    routed_part = jnp.einsum(
        "scd,sgfd->sgcf", slot_inputs, expert_gate_up, preferred_element_type=jnp.float32
    )
    shared_part = jnp.einsum(
        "td,gfd->gtf", column_rows, shared_gate_up, preferred_element_type=jnp.float32
    )
    routed_sum, shared_sum = lax.psum((routed_part, shared_part), "dp")
    activated = (jax.nn.silu(routed_sum[:, 0]) * routed_sum[:, 1]).astype(jnp.bfloat16)
    slot_out = jnp.einsum(
        "scf,sfd->scd", activated, expert_down, preferred_element_type=jnp.float32
    )
    routed = jnp.einsum("tsc,scd->td", combine, slot_out, precision=HIGHEST)
    shared_act = (jax.nn.silu(shared_sum[0]) * shared_sum[1]).astype(jnp.bfloat16)
    shared_term = jnp.dot(shared_act, shared_down, preferred_element_type=jnp.float32)
    moe_rows = lax.psum_scatter(routed, "expert", scatter_dimension=0, tiled=True)
    moe_part = lax.all_to_all(moe_rows + shared_term, "dp", split_axis=0, concat_axis=1, tiled=True)
    layer_out = (residual + moe_part).astype(jnp.bfloat16)
    changed = old_place != new_place
    moved_slot = jnp.argmax(changed, axis=1)
    wanted_expert = jnp.take_along_axis(new_place, moved_slot[:, None], axis=1)[:, 0]
    source = holder[wanted_expert]
    stacked_gate_up = expert_gate_up.reshape(slots_local, 2 * ff_width, col_width)
    spread = (
        lax.all_to_all(stacked_gate_up, "expert", split_axis=1, concat_axis=0, tiled=True),
        lax.all_to_all(expert_down, "expert", split_axis=1, concat_axis=0, tiled=True),
    )
    outgoing = (spread[0][source], spread[1][source])
    arrived = (
        lax.all_to_all(outgoing[0], "expert", split_axis=0, concat_axis=1, tiled=True),
        lax.all_to_all(outgoing[1], "expert", split_axis=0, concat_axis=1, tiled=True),
    )
    arrived_gate_up = arrived[0].reshape(1, 2, ff_width, col_width)
    my_slot = moved_slot[ex_index]
    is_moved = jnp.arange(slots_local, dtype=jnp.int32) == my_slot
    moved_gate_up = jnp.where(is_moved[:, None, None, None], arrived_gate_up, expert_gate_up)
    moved_down = jnp.where(is_moved[:, None, None], arrived[1], expert_down)
    return (layer_out, moved_gate_up, moved_down)


def solution(mesh):
    in_specs = (
        P(("dp", "expert"), None),
        P(),
        P("expert", None),
        P(),
        P(None, "expert"),
        P("expert", None),
        P("dp", None, None),
        P(),
        P(),
        P(),
        P(),
        P(),
        P(),
        P(),
        P("expert", None, None, "dp"),
        P("expert", None, "dp"),
        P(None, None, "dp"),
        P(None, "dp"),
    )
    out_specs = (P(("dp", "expert"), None), P("expert", None, None, "dp"), P("expert", None, "dp"))
    return jax.shard_map(local, mesh=mesh, in_specs=in_specs, out_specs=out_specs, check_vma=False)
```

profile of v0, /device:TPU:0, one launch (start us, length us, event | category | flops | bytes accessed | tf_op | source)
XLA Modules:
  0.0 888.6 jit_solution(454954826351109402)
XLA Ops:
  8.4 2.4 scatter_custom_fusion
  12.6 44.5 %all-gather.3 = bf16[32,1,2048]{2,1,0:T(2,128)(2,1)S(1)} all-gather(bf16[1,1,2048]{2,1,0:T(2,128)(2,1)} %bitcast.231), channel_id=1, replica_groups=mesh['dp'=4,'expert'=8] {'dp','expert'}, dimensions={0}, use_global_device_ids=true | all-gather | bytes 135168 | tf_op jit(solution)/shard_map/all_gather | solution.py:98
  59.0 2.0 fusion.86
  68.4 1.6 fusion.9
  74.7 1.5 convolution_multiply_fusion
  76.5 9.4 %all-gather.2 = f32[128,2,512]{2,0,1:T(8,128)S(1)} all-gather(f32[32,2,512]{2,0,1:T(8,128)S(1)} %fusion.24), channel_id=4, replica_groups=mesh['dp'=4,'expert'=8] {'dp'}, dimensions={0}, use_global_device_ids=true | all-gather | bytes 655360 | tf_op jit(solution)/shard_map/all_gather | solution.py:23
  86.2 8.6 all-gather.5
  96.0 7.6 all-gather.4
  104.8 13.2 %while.19 = (s32[]{:T(128)}, f32[32,2]{0,1:T(2,128)}, f32[32,2]{0,1:T(2,128)}, f32[32,2,512]{2,1,0:T(2,128)S(1)}, f32[4,32,2]{1,2,0:T(2,128)}, /*index=5*/f32[4,...) while((s32[]{:T(128)}, f32[32,2]{0,1:T(2,128)}, f32[32,2]{0,1:T(2,128)}, ...), condition=%wide.region_6.7_spmd, body=%wide.region_5.6_spmd.sunk | while | flops 98693 | bytes 659095 | solution.py:28
  106.9 1.3 copy.204
  109.2 1.3 fusion.103
  111.3 1.3 copy.204
  113.7 1.3 fusion.103
  115.7 1.3 copy.204
  118.1 2.5 fusion.29
  123.0 1.4 fusion.78
  125.3 1.3 fusion.69
  126.7 1.3 copy.134
  130.2 2.3 fusion.11
  136.4 4.4 compare_select_fusion.3
  140.9 10.5 %select_subtract_fusion = s32[192]{0:T(256)S(1)} fusion(pred[192]{0:T(512)(128)(4,1)S(1)} %get-tuple-element.241, pred[192]{0:T(512)(128)(4,1)S(1)} %get-tuple-element.240, pred[192]{0:T(512)(128)(4,1)S(1)} %get-tuple-element.239, pred[192]{0:T(512)(128)(4,1)S(1)} %get-tuple-element.238, pred[192]{0:T(512)(128)(4,1)S(1)} %get-tuple-element.237, ...), kind=kLoop, calls=%fused_computation.178 | loop fusion | flops 3456 | bytes 4872 | tf_op jit(solution)/shard_map/sub | solution.py:210
  155.6 28.0 %all-reduce.8.cloned.1.call-done = f32[8,2048]{1,0:T(8,128)} async-done(((f32[8,2048]{1,0:T(8,128)}), f32[8,2048]{1,0:T(8,128)}) %all-reduce.8.cloned.1.call-update) | async-done | bytes 65552
  183.6 2.1 multiply_reduce_fusion.1
  187.1 40.5 %all-gather.6 = bf16[32,1,2048]{2,1,0:T(2,128)(2,1)S(1)} all-gather(bf16[1,1,2048]{2,1,0:T(2,128)(2,1)S(1)} %convert_bitcast_fusion), channel_id=1, replica_groups=mesh['dp'=4,'expert'=8] {'dp','expert'}, dimensions={0}, use_global_device_ids=true | all-gather | bytes 135168 | tf_op jit(solution)/shard_map/all_gather | solution.py:186
  227.8 4.9 convolution_bitcast_fusion
  232.7 6.9 convolution_bitcast_fusion.1
  239.6 45.8 %all-reduce.12.cloned.1.call-done = (f32[2,4,2816]{2,1,0:T(4,128)}, f32[4,2,16,1408]{3,2,1,0:T(8,128)}) async-done(((f32[2,4,2816]{2,1,0:T(4,128)}, f32[4,2,16,1408]{3,2,1,0:T(8,128)}), (f32[2,4,2816]{2,1,0:T(4,128)}, f32[4,2,16,1408]{3,2,1,0:T(8,128)})) %all-reduce.12.cloned.1.call-update) | async-done | bytes 811024 | tf_op jit(solution)/shard_map/psum | solution.py:229
  285.4 3.8 fusion.21
  290.8 53.2 %all-reduce.10.cloned.1.call-done = f32[32,512]{1,0:T(8,128)} async-done(((f32[32,512]{1,0:T(8,128)}), f32[32,512]{1,0:T(8,128)}) %all-reduce.10.cloned.1.call-update) | async-done | bytes 65552
  345.8 3.6 all-to-all-start
  349.4 23.9 %copy.152 = bf16[4,1408,512]{2,0,1:T(4,128)(2,1)} copy(bf16[4,1408,512]{2,1,0:T(8,128)(2,1)} %param.35) | data formatting | bytes 11534336 | tf_op args[15]
  373.3 4.7 all-to-all-start.3
  378.0 14.4 %copy.149 = bf16[4,2,1408,512]{3,0,2,1:T(4,128)(2,1)} copy(bf16[4,2,1408,512]{3,2,1,0:T(8,128)(2,1)} %param.34) | data formatting | bytes 23068672 | tf_op args[14]
  392.4 113.3 %all-to-all-done.3 = bf16[4,1408,512]{2,0,1:T(4,128)(2,1)} async-done(((bf16[4,1408,512]{2,0,1:T(4,128)(2,1)}), bf16[4,1408,512]{2,0,1:T(4,128)(2,1)}, u32[]{:S(2)}, u32[]{:S(2)}) %all-to-all-start.3) | async-done | bytes 5767200 | tf_op jit(solution)/shard_map/all_to_all | solution.py:247
  505.7 5.4 all-to-all-start.1
  513.0 3.8 copy.153
  516.8 2.9 copy.154
  519.7 4.4 gather_fusion.5
  524.1 238.3 %all-to-all-done.1 = bf16[4,2816,512]{2,0,1:T(4,128)(2,1)} async-done(((bf16[4,2816,512]{2,0,1:T(4,128)(2,1)}), bf16[4,2816,512]{2,0,1:T(4,128)(2,1)}, u32[]{:S(2)}, u32[]{:S(2)}) %all-to-all-start.1) | async-done | bytes 11534368 | tf_op jit(solution)/shard_map/all_to_all | solution.py:246
  762.4 3.6 all-to-all-start.4
  766.0 7.9 copy.150
  773.9 5.1 copy.151
  779.0 6.6 gather_fusion.4
  785.6 15.4 %all-to-all-done.4 = bf16[8,176,512]{2,1,0:T(8,128)(2,1)S(1)} async-done(((bf16[8,176,512]{2,1,0:T(8,128)(2,1)}), bf16[8,176,512]{2,1,0:T(8,128)(2,1)S(1)}, u32[]{:S(2)}, u32[]{:S(2)}) %all-to-all-start.4) | async-done | bytes 1441824 | tf_op jit(solution)/shard_map/all_to_all | solution.py:252
  800.9 4.4 all-to-all-start.2
  807.2 5.8 broadcast_select_fusion.1
  813.0 58.2 %all-to-all-done.2 = bf16[8,352,512]{2,1,0:T(8,128)(2,1)} async-done(((bf16[8,352,512]{2,1,0:T(8,128)(2,1)}), bf16[8,352,512]{2,1,0:T(8,128)(2,1)}, u32[]{:S(2)}, u32[]{:S(2)}) %all-to-all-start.2) | async-done | bytes 2883616 | tf_op jit(solution)/shard_map/all_to_all | solution.py:251
  871.3 10.8 %broadcast_select_fusion = bf16[4,2,1408,512]{3,2,1,0:T(8,128)(2,1)} fusion(bf16[4,2,1408,512]{3,2,1,0:T(8,128)(2,1)} %param.34, pred[4]{0:T(512)(128)(4,1)S(1)} %iota_compare_fusion.7, bf16[2,1408,512]{2,1,0:T(8,128)(2,1)} %bitcast.74), kind=kLoop, calls=%fused_computation.19 | loop fusion | flops 5767168 | bytes 25952260 | tf_op jit(solution)/shard_map/jit(_where)/select_n | solution.py:257
  (152 shorter events, 47.4 us)
Async XLA Ops:
  7.2 336.8 %copy-start = (bf16[2816,512]{1,0:T(8,128)(2,1)S(1)}, bf16[2816,512]{1,0:T(8,128)(2,1)}, u32[]{:S(2)}) copy-start(bf16[2816,512]{1,0:T(8,128)(2,1)} %param.37) | copy-start | bytes 8650756
  7.2 53.9 %copy-start.15 = (s32[32]{0:T(128)S(1)}, s32[32]{0:T(128)}, u32[]{:S(2)}) copy-start(s32[32]{0:T(128)} %param.28) | copy-start | bytes 388
  7.2 176.4 %all-reduce.8.cloned.1.call-start = ((), (), s32[]{:S(2)}) async-start(), calls=%async_computation.5 | async-start | bytes 131072
  7.3 58.0 %copy-start.14 = (f32[32]{0:T(128)}, f32[32]{0:T(128)S(1)}, u32[]{:S(2)}) copy-start(f32[32]{0:T(128)S(1)} %multiply_exponential_fusion) | copy-start | bytes 388
  11.5 0.5 copy-start.10
  58.4 0.7 copy-start.5
  63.0 13.2 %copy-start.3 = (bf16[512,512]{0,1:T(8,128)(2,1)}, bf16[512,512]{0,1:T(8,128)(2,1)S(1)}, u32[]{:S(2)}) copy-start(bf16[512,512]{0,1:T(8,128)(2,1)S(1)} %copy.126) | copy-start | bytes 1572868
  66.2 0.6 copy-start.7
  66.2 0.6 copy-start.8
  68.4 7.8 copy-start.11
  71.3 14.6 %copy-start.12 = (s32[32]{0:T(128)S(1)}, s32[32]{0:T(128)}, u32[]{:S(2)}) copy-start(s32[32]{0:T(128)} %copy-done.10) | copy-start | bytes 388
  118.1 12.1 %copy-start.4 = (bf16[512,512]{0,1:T(8,128)(2,1)S(1)}, bf16[512,512]{0,1:T(8,128)(2,1)}, u32[]{:S(2)}) copy-start(bf16[512,512]{0,1:T(8,128)(2,1)} %copy-done.3) | copy-start | bytes 1572868
  120.5 0.6 copy-start.6
  132.5 153.0 %all-reduce.12.cloned.1.call-start = ((), (), s32[]{:S(2)}) async-start(), calls=%async_computation.7 | async-start | bytes 1622016 | tf_op jit(solution)/shard_map/psum | solution.py:229
  239.6 104.4 %all-reduce.10.cloned.1.call-start = ((), (), s32[]{:S(2)}) async-start(), calls=%async_computation.6 | async-start | bytes 131072
  285.4 58.5 %copy-start.9 = (f32[2,4,2816]{2,1,0:T(4,128)S(1)}, f32[2,4,2816]{2,1,0:T(4,128)}, u32[]{:S(2)}) copy-start(f32[2,4,2816]{2,1,0:T(4,128)} %get-tuple-element.256) | copy-start | bytes 270340
  345.8 27.5 %all-to-all-start = ((f32[4,1,512]{2,1,0:T(1,128)}), f32[4,1,512]{2,1,0:T(1,128)S(1)}, u32[]{:S(2)}, u32[]{:S(2)}) async-start(f32[4,1,512]{2,1,0:T(1,128)} %copy.148), calls=%async_computation | async-start | bytes 16384 | tf_op jit(solution)/shard_map/all_to_all | solution.py:238
  373.3 132.4 %all-to-all-start.3 = ((bf16[4,1408,512]{2,0,1:T(4,128)(2,1)}), bf16[4,1408,512]{2,0,1:T(4,128)(2,1)}, u32[]{:S(2)}, u32[]{:S(2)}) async-start(bf16[4,1408,512]{2,0,1:T(4,128)(2,1)} %copy.152), calls=%async_computation.3 | async-start | bytes 11534336 | tf_op jit(solution)/shard_map/all_to_all | solution.py:247
  505.7 5.4 copy-start.2
  505.7 5.4 copy-start.13
  505.7 256.7 %all-to-all-start.1 = ((bf16[4,2816,512]{2,0,1:T(4,128)(2,1)}), bf16[4,2816,512]{2,0,1:T(4,128)(2,1)}, u32[]{:S(2)}, u32[]{:S(2)}) async-start(bf16[4,2816,512]{2,0,1:T(4,128)(2,1)} %bitcast.217), calls=%async_computation.1 | async-start | bytes 23068672 | tf_op jit(solution)/shard_map/all_to_all | solution.py:246
  762.4 38.5 %all-to-all-start.4 = ((bf16[8,176,512]{2,1,0:T(8,128)(2,1)}), bf16[8,176,512]{2,1,0:T(8,128)(2,1)S(1)}, u32[]{:S(2)}, u32[]{:S(2)}) async-start(bf16[8,176,512]{2,1,0:T(8,128)(2,1)} %gather_fusion.5), calls=%async_computation.4 | async-start | bytes 2883584 | tf_op jit(solution)/shard_map/all_to_all | solution.py:252
  800.9 70.4 %all-to-all-start.2 = ((bf16[8,352,512]{2,1,0:T(8,128)(2,1)}), bf16[8,352,512]{2,1,0:T(8,128)(2,1)}, u32[]{:S(2)}, u32[]{:S(2)}) async-start(bf16[8,352,512]{2,1,0:T(8,128)(2,1)} %gather_fusion.4), calls=%async_computation.2 | async-start | bytes 5767168 | tf_op jit(solution)/shard_map/all_to_all | solution.py:251
  871.3 10.8 %copy-start.1 = (bf16[2816,512]{1,0:T(8,128)(2,1)S(1)}, bf16[2816,512]{1,0:T(8,128)(2,1)}, u32[]{:S(2)}) copy-start(bf16[2816,512]{1,0:T(8,128)(2,1)} %param.37) | copy-start | bytes 8650756
Sparse Core Ops, SparseCore 0:
  132.6 50.9 all-reduce.7
  239.7 45.7 all-reduce.11
  290.2 53.6 all-reduce.9
where the time goes:
time: 891 us; the launch traced here: 889 us
  waiting for transfers between devices  552 us (62%)
  blocking collectives  111 us (12%)
  local copies, waits for them, and re-layouts  100 us (11%)
  other arithmetic  57 us (6%)
  matrix products  31 us (3%)
  starting transfers between devices  21.9 us (2%)
  between operations  15.6 us (2%)
    all_to_all x1, waiting for transfers between devices, local(): lax.all_to_all(stacked_gate_up, 'expert', split_axis=1, concat_axis=0, ti...  238 us
    all_to_all x1, waiting for transfers between devices, local(): lax.all_to_all(expert_down, 'expert', split_axis=1, concat_axis=0, tiled=...  113 us
    unnamed x5, waiting for transfers between devices  81.2 us
    all_to_all x1, waiting for transfers between devices, local(): lax.all_to_all(outgoing[0], 'expert', split_axis=0, concat_axis=1, tiled=...  58.2 us
    psum x1, waiting for transfers between devices, local(): routed_sum, shared_sum = lax.psum((routed_part, shared_part), 'dp')  45.8 us
    unnamed x41, local copies, waits for them, and re-layouts  44.8 us
    all_gather x1, blocking collectives, local(): everyone = lax.all_gather(hidden, ('dp', 'expert'), axis=0, tiled=True)  44.5 us
    all_gather x1, blocking collectives, local(): every_row = lax.all_gather(normed_ffn, ('dp', 'expert'), axis=0, tiled=True)  40.5 us
  transfers between devices with their start and end apart: 8, of which 7 were waited for; matrix products, arithmetic and copies ran while one was open for 11% of the time, Pallas kernels for 0%

commit v1 on v0

--- a/solution.py
+++ b/solution.py
@@ -17,17 +17,6 @@
 ROPE_BASE = 50000.0
 MASKED_SCORE = -1e30
 HIGHEST = lax.Precision.HIGHEST
-
-
-def combined_all(part, axis, combine):
-    gathered = jax.tree.map(lambda a: lax.all_gather(a, axis), part)
-
-    def take(source):
-        return jax.tree.map(lambda a: lax.dynamic_index_in_dim(a, source, 0, False), gathered)
-
-    return lax.fori_loop(
-        1, lax.axis_size(axis), lambda source, state: combine(state, take(source)), take(0)
-    )
 
 
 def rms_plain(values):
@@ -54,15 +43,68 @@
     )
 
 
-def combine_parts(earlier, later):
-    highest = jnp.maximum(earlier[0], later[0])
-    weight_early = jnp.exp(earlier[0] - highest)
-    weight_late = jnp.exp(later[0] - highest)
-    return (
-        highest,
-        earlier[1] * weight_early + later[1] * weight_late,
-        earlier[2] * weight_early[..., None] + later[2] * weight_late[..., None],
-    )
+def gather_rows(rows):
+    by_expert = lax.all_gather(rows, "expert", axis=0, tiled=True)
+    return lax.all_gather(by_expert, "dp", axis=0, tiled=True)
+
+
+def spread_slots(gate_up, down, picks, ex_count):
+    chosen = jnp.concatenate([gate_up[picks], down[picks][:, None]], axis=1)
+    count, parts, ff_width, col_width = chosen.shape
+    pieces = chosen.reshape(count, parts, ex_count, ff_width // ex_count, col_width)
+    spread = lax.all_to_all(pieces, "expert", split_axis=2, concat_axis=0, tiled=True)
+    return spread.reshape(ex_count * count, parts, ff_width // ex_count, col_width)
+
+
+def migrate(expert_gate_up, expert_down, old_place, new_place, ex_index):
+    rows, slots_local = old_place.shape
+    slots = rows * slots_local
+    ex_count = rows
+    ff_width = expert_gate_up.shape[2]
+    changed = old_place != new_place
+    moved_slot = jnp.argmax(changed, axis=1)
+    wanted = jnp.take_along_axis(new_place, moved_slot[:, None], axis=1)[:, 0]
+    hit = old_place.reshape(-1)[None, :] == wanted[:, None]
+    first = jnp.argmax(hit, axis=1).astype(jnp.int32)
+    last = (slots - 1 - jnp.argmax(hit[:, ::-1], axis=1)).astype(jnp.int32)
+    slot_ids = jnp.arange(slots, dtype=jnp.int32)
+
+    def needed_of(src):
+        needed = jnp.any(src[:, None] == slot_ids[None, :], axis=0).reshape(rows, slots_local)
+        return needed, jnp.max(jnp.sum(needed.astype(jnp.int32), axis=1))
+
+    need_first, load_first = needed_of(first)
+    need_last, load_last = needed_of(last)
+    use_last = load_last < load_first
+    source = jnp.where(use_last, last, first)
+    needed = jnp.where(use_last, need_last, need_first)
+    load = jnp.minimum(load_first, load_last)
+    rank = jnp.cumsum(needed.astype(jnp.int32), axis=1) - 1
+    local_ids = jnp.arange(slots_local, dtype=jnp.int32)
+    picks = jnp.stack(
+        [jnp.argmax(needed & (rank == k), axis=1).astype(jnp.int32) for k in range(slots_local)],
+        axis=1,
+    )
+    my_picks = picks[ex_index]
+    src_dev = source // slots_local
+    src_rank = rank.reshape(-1)[source]
+    fast = min(2, slots_local)
+    spread_a = spread_slots(expert_gate_up, expert_down, my_picks[:fast], ex_count)
+    out_a = spread_a[src_dev * fast + jnp.minimum(src_rank, fast - 1)]
+    if slots_local > fast:
+        rest = slots_local - fast
+
+        def extra():
+            spread_b = spread_slots(expert_gate_up, expert_down, my_picks[fast:], ex_count)
+            return spread_b[src_dev * rest + jnp.clip(src_rank - fast, 0, rest - 1)]
+
+        out_b = lax.cond(load > fast, extra, lambda: jnp.zeros_like(out_a))
+        out_a = jnp.where((src_rank < fast)[:, None, None, None], out_a, out_b)
+    arrived = lax.all_to_all(out_a, "expert", split_axis=0, concat_axis=2, tiled=True)
+    is_moved = local_ids == moved_slot[ex_index]
+    moved_gate_up = jnp.where(is_moved[:, None, None, None], arrived[:, :2], expert_gate_up)
+    moved_down = jnp.where(is_moved[:, None, None], arrived[:, 2], expert_down)
+    return moved_gate_up, moved_down
 
 
 def local(
@@ -95,7 +137,7 @@
     head_local = query_weight.shape[0] // (NOPE + ROPE)
     score_scale = (NOPE + ROPE) ** (-0.5)
     group_start = dp_index * group_rows
-    everyone = lax.all_gather(hidden, ("dp", "expert"), axis=0, tiled=True)
+    everyone = gather_rows(hidden)
     normed = rms_norm(everyone.astype(jnp.float32), attn_gain).astype(jnp.bfloat16)
     queries = jnp.einsum(
         "td,qd->tq", normed, query_weight, preferred_element_type=jnp.float32
@@ -147,10 +189,14 @@
     req_mix = jnp.einsum(
         "rp,phl->rhl", member_float, page_mix * rescale[..., None], precision=HIGHEST
     )
-    merged = combined_all((req_max, req_total, req_mix), "dp", combine_parts)
-    part_max = lax.dynamic_slice_in_dim(merged[0], group_start, group_rows, 0)
-    part_total = lax.dynamic_slice_in_dim(merged[1], group_start, group_rows, 0)
-    part_mix = lax.dynamic_slice_in_dim(merged[2], group_start, group_rows, 0)
+    packed = jnp.concatenate([req_mix, req_max[..., None], req_total[..., None]], axis=-1)
+    gathered = lax.all_gather(packed, "dp", axis=0, tiled=False)
+    gathered = lax.dynamic_slice_in_dim(gathered, group_start, group_rows, 1)
+    each_max = gathered[..., LATENT]
+    part_max = jnp.max(each_max, axis=0)
+    each_weight = jnp.exp(each_max - part_max[None])
+    part_total = jnp.sum(gathered[..., LATENT + 1] * each_weight, axis=0)
+    part_mix = jnp.sum(gathered[..., :LATENT] * each_weight[..., None], axis=0)
     own_normed = lax.dynamic_slice_in_dim(normed, group_start, group_rows, 0)
     own_position = lax.dynamic_slice_in_dim(position, group_start, group_rows, 0)
     fresh_latent = jnp.dot(own_normed, latent_down, preferred_element_type=jnp.float32)
@@ -183,7 +229,7 @@
     slots_local = expert_gate_up.shape[0]
     ff_width = expert_gate_up.shape[2]
     col_width = expert_gate_up.shape[3]
-    every_row = lax.all_gather(normed_ffn, ("dp", "expert"), axis=0, tiled=True)
+    every_row = gather_rows(normed_ffn)
     my_columns = lax.dynamic_slice_in_dim(every_row, dp_index * col_width, col_width, 1)
     by_group = my_columns.reshape(dp_count, ex_count, req_local, col_width).transpose(1, 0, 2, 3)
     ffn_rows = by_group.reshape(requests, col_width)
@@ -237,25 +283,7 @@
     moe_rows = lax.psum_scatter(routed, "expert", scatter_dimension=0, tiled=True)
     moe_part = lax.all_to_all(moe_rows + shared_term, "dp", split_axis=0, concat_axis=1, tiled=True)
     layer_out = (residual + moe_part).astype(jnp.bfloat16)
-    changed = old_place != new_place
-    moved_slot = jnp.argmax(changed, axis=1)
-    wanted_expert = jnp.take_along_axis(new_place, moved_slot[:, None], axis=1)[:, 0]
-    source = holder[wanted_expert]
-    stacked_gate_up = expert_gate_up.reshape(slots_local, 2 * ff_width, col_width)
-    spread = (
-        lax.all_to_all(stacked_gate_up, "expert", split_axis=1, concat_axis=0, tiled=True),
-        lax.all_to_all(expert_down, "expert", split_axis=1, concat_axis=0, tiled=True),
-    )
-    outgoing = (spread[0][source], spread[1][source])
-    arrived = (
-        lax.all_to_all(outgoing[0], "expert", split_axis=0, concat_axis=1, tiled=True),
-        lax.all_to_all(outgoing[1], "expert", split_axis=0, concat_axis=1, tiled=True),
-    )
-    arrived_gate_up = arrived[0].reshape(1, 2, ff_width, col_width)
-    my_slot = moved_slot[ex_index]
-    is_moved = jnp.arange(slots_local, dtype=jnp.int32) == my_slot
-    moved_gate_up = jnp.where(is_moved[:, None, None, None], arrived_gate_up, expert_gate_up)
-    moved_down = jnp.where(is_moved[:, None, None], arrived[1], expert_down)
+    moved_gate_up, moved_down = migrate(expert_gate_up, expert_down, old_place, new_place, ex_index)
     return (layer_out, moved_gate_up, moved_down)
 
 

time: 891 us -> 694 us (0.78)
  waiting for transfers between devices: 552 us -> 228 us
  blocking collectives: 111 us -> 238 us
  other arithmetic: 57 us -> 79.7 us
  local copies, waits for them, and re-layouts: 100 us -> 79.7 us
    all_to_all x4 -> x2, waiting for transfers between devices: 425 us -> 95 us  [the longest x1 95 us: migrate(): lax.all_to_all(out_a, 'expert', split_axis=0, concat_axis=2, tiled=True)]
    all_gather x5, blocking collectives: 111 us -> 238 us  [the longest x2 210 us: gather_rows(): by_expert = lax.all_gather(rows, 'expert', axis=0, tiled=True)]
    unnamed x41 -> x73, local copies, waits for them, and re-layouts: 44.8 us -> 10.5 us
    gather x4 -> x8, local copies, waits for them, and re-layouts: 12.3 us -> 34.7 us  [the longest x5 25.9 us: spread_slots(): chosen = jnp.concatenate([gate_up[picks], down[picks][:, None]], axis=1)]
    all_to_all x4 -> x1, local copies, waits for them, and re-layouts: 19.7 us -> 2.5 us  [migrate(): lax.all_to_all(out_a, 'expert', split_axis=0, concat_axis=2, tiled=True)]
    all_to_all x4 -> x2, starting transfers between devices: 18.1 us -> 11 us  [the longest x1 6.46 us: spread_slots(): lax.all_to_all(pieces, 'expert', split_axis=2, concat_axis=0, tiled=True)]
    select_n x4 -> x8, other arithmetic: 16.6 us -> 21.5 us  [the longest x1 11 us: migrate(): jnp.where(is_moved[:, None, None, None], arrived[:, :2], expert_gate_up)]
  transfers between devices with their start and end apart: 8 -> 6, of which waited for: 7 -> 4; matrix products, arithmetic and copies ran while one was open for 11% -> 16% of each run, Pallas kernels for 0% -> 0%
where the time goes in v1:
time: 694 us; the launch traced here: 692 us
  blocking collectives  238 us (34%)
  waiting for transfers between devices  228 us (33%)
  local copies, waits for them, and re-layouts  79.7 us (11%)
  other arithmetic  79.7 us (11%)
  matrix products  33.6 us (5%)
  between operations  18.1 us (3%)
  starting transfers between devices  14.8 us (2%)
    all_gather x2, blocking collectives, gather_rows(): by_expert = lax.all_gather(rows, 'expert', axis=0, tiled=True)  210 us
    all_to_all x1, waiting for transfers between devices, migrate(): lax.all_to_all(out_a, 'expert', split_axis=0, concat_axis=2, tiled=True)  95 us
    unnamed x5, waiting for transfers between devices  86.1 us
    psum x1, waiting for transfers between devices, local(): routed_sum, shared_sum = lax.psum((routed_part, shared_part), 'dp')  46.9 us
    gather x5, local copies, waits for them, and re-layouts, spread_slots(): chosen = jnp.concatenate([gate_up[picks], down[picks][:, None]], axis=1)  25.9 us
    all_gather x2, blocking collectives, gather_rows(): return lax.all_gather(by_expert, 'dp', axis=0, tiled=True)  16.9 us
  transfers between devices with their start and end apart: 6, of which 4 were waited for; matrix products, arithmetic and copies ran while one was open for 16% of the time, Pallas kernels for 0%

profile of v1, /device:TPU:0, one launch (start us, length us, event | category | flops | bytes accessed | tf_op | source)
XLA Modules:
  0.0 691.6 jit_solution(8807751896408755276)
XLA Ops:
  18.1 5.9 mini-gather-slice.2
  24.0 5.2 mini-gather-slice.3
  30.6 5.2 gather_fusion.11
  35.8 4.7 gather_fusion.12
  40.5 5.0 gather_fusion.8
  45.5 5.6 pad_maximum_fusion.3
  51.1 7.7 %pad_maximum_fusion.2 = bf16[2,3,8,176,512]{4,3,2,1,0:T(8,128)(2,1)} fusion(bf16[2,1,8,176,512]{4,3,2,1,0:T(8,128)(2,1)} %bitcast.229, bf16[2,2,8,176,512]{4,3,2,1,0:T(8,128)(2,1)} %bitcast.225), kind=kLoop, calls=%fused_computation.22 | loop fusion | flops 4325376 | bytes 17301504 | tf_op jit(solution)/shard_map/concatenate | solution.py:52
  58.8 7.6 %copy.166 = bf16[2,3,8,176,512]{4,3,1,0,2:T(8,128)(2,1)} copy(bf16[2,3,8,176,512]{4,3,2,1,0:T(8,128)(2,1)} %pad_maximum_fusion.2) | data formatting | bytes 17301504 | tf_op jit(solution)/shard_map/concatenate | solution.py:52
  68.7 2.5 conditional.1
  68.7 2.5 broadcast.321
  71.3 6.5 all-to-all-start.2
  77.8 195.6 %all-gather.1 = bf16[8,1,2048]{2,1,0:T(2,128)(2,1)S(1)} all-gather(bf16[1,1,2048]{2,1,0:T(2,128)(2,1)S(1)} %bitcast.240), channel_id=1, replica_groups=mesh['dp'=4,'expert'=8] {'expert'}, dimensions={0}, use_global_device_ids=true | all-gather | bytes 36864 | tf_op jit(solution)/shard_map/all_gather | solution.py:47
  273.4 8.5 %all_gather.19 = bf16[32,2048]{1,0:T(8,128)(2,1)S(1)} all-gather(bf16[8,2048]{1,0:T(8,128)(2,1)S(1)} %bitcast.236), channel_id=1, replica_groups=mesh['dp'=4,'expert'=8] {'dp'}, dimensions={0}, use_global_device_ids=true | all-gather | bytes 163840 | tf_op jit(solution)/shard_map/all_gather | solution.py:48
  282.2 2.0 fusion.91
  289.1 2.6 scatter_custom_fusion
  297.2 2.3 gather_fusion.4
  299.4 1.6 fusion.6
  301.0 1.9 fusion.90
  304.2 1.4 copy.148
  311.3 1.4 convolution_bitcast_fusion.3
  312.7 1.4 copy.152
  314.0 1.3 copy.151
  316.7 1.6 convolution_multiply_fusion
  320.0 11.4 %all-gather = f32[128,2,514]{2,0,1:T(8,128)S(1)} all-gather(f32[32,2,514]{2,0,1:T(8,128)S(1)} %pad_maximum_fusion.4), channel_id=2, replica_groups=mesh['dp'=4,'expert'=8] {'dp'}, dimensions={0}, use_global_device_ids=true | all-gather | bytes 657920 | tf_op jit(solution)/shard_map/all_gather | solution.py:193
  333.8 1.5 copy.183
  335.2 2.4 fusion.26
  343.7 1.7 copy.181
  345.4 3.0 multiply_reduce_fusion
  350.0 2.4 fusion.8
  354.8 4.5 compare_select_fusion.5
  359.4 10.5 %select_subtract_fusion = s32[192]{0:T(256)S(1)} fusion(pred[192]{0:T(512)(128)(4,1)S(1)} %get-tuple-element.86, pred[192]{0:T(512)(128)(4,1)S(1)} %get-tuple-element.85, pred[192]{0:T(512)(128)(4,1)S(1)} %get-tuple-element.84, pred[192]{0:T(512)(128)(4,1)S(1)} %get-tuple-element.83, pred[192]{0:T(512)(128)(4,1)S(1)} %get-tuple-element.82, ...), kind=kLoop, calls=%fused_computation.212 | loop fusion | flops 3456 | bytes 4872 | tf_op jit(solution)/shard_map/sub | solution.py:256
  372.7 32.9 %all-reduce.8.cloned.1.call-done = f32[8,2048]{1,0:T(8,128)} async-done(((f32[8,2048]{1,0:T(8,128)}), f32[8,2048]{1,0:T(8,128)}) %all-reduce.8.cloned.1.call-update) | async-done | bytes 65552
  405.6 2.1 multiply_reduce_fusion.2
  408.4 14.0 %all-gather.2 = bf16[8,1,2048]{2,1,0:T(2,128)(2,1)S(1)} all-gather(bf16[1,1,2048]{2,1,0:T(2,128)(2,1)S(1)} %convert_bitcast_fusion), channel_id=1, replica_groups=mesh['dp'=4,'expert'=8] {'expert'}, dimensions={0}, use_global_device_ids=true | all-gather | bytes 36864 | tf_op jit(solution)/shard_map/all_gather | solution.py:47
  422.4 8.4 %all_gather.23 = bf16[32,2048]{1,0:T(8,128)(2,1)S(1)} all-gather(bf16[8,2048]{1,0:T(8,128)(2,1)S(1)} %bitcast.237), channel_id=1, replica_groups=mesh['dp'=4,'expert'=8] {'dp'}, dimensions={0}, use_global_device_ids=true | all-gather | bytes 163840 | tf_op jit(solution)/shard_map/all_gather | solution.py:48
  430.9 4.9 convolution_bitcast_fusion
  435.8 6.9 convolution_bitcast_fusion.1
  443.4 46.9 %all-reduce.12.cloned.1.call-done = (f32[2,4,2816]{2,1,0:T(4,128)}, f32[4,2,16,1408]{3,2,1,0:T(8,128)}) async-done(((f32[2,4,2816]{2,1,0:T(4,128)}, f32[4,2,16,1408]{3,2,1,0:T(8,128)}), (f32[2,4,2816]{2,1,0:T(4,128)}, f32[4,2,16,1408]{3,2,1,0:T(8,128)})) %all-reduce.12.cloned.1.call-update) | async-done | bytes 811024 | tf_op jit(solution)/shard_map/psum | solution.py:275
  490.3 3.8 fusion.18
  495.6 53.1 %all-reduce.10.cloned.1.call-done = f32[32,512]{1,0:T(8,128)} async-done(((f32[32,512]{1,0:T(8,128)}), f32[32,512]{1,0:T(8,128)}) %all-reduce.10.cloned.1.call-update) | async-done | bytes 65552
  550.6 3.6 all-to-all-start.1
  554.2 6.3 gather_fusion.9
  560.6 6.1 broadcast_select_fusion.2
  566.7 4.6 all-to-all-start.3
  573.1 95.0 %all-to-all-done.3 = bf16[8,3,176,512]{3,2,1,0:T(8,128)(2,1)} async-done(((bf16[8,3,176,512]{3,2,1,0:T(8,128)(2,1)}), bf16[8,3,176,512]{3,2,1,0:T(8,128)(2,1)}, u32[]{:S(2)}, u32[]{:S(2)}) %all-to-all-start.3) | async-done | bytes 4325408 | tf_op jit(solution)/shard_map/all_to_all | solution.py:103
  668.1 2.5 copy.168
  670.9 11.0 %broadcast_select_fusion = bf16[4,2,1408,512]{3,2,1,0:T(8,128)(2,1)} fusion(bf16[4,2,1408,512]{3,2,1,0:T(8,128)(2,1)} %param.34, pred[4]{0:T(512)(128)(4,1)S(1)} %iota_compare_fusion.9, bf16[2,1408,512]{2,1,0:T(8,128)(2,1)S(1)} %slice_bitcast_fusion), kind=kLoop, calls=%fused_computation.21 | loop fusion | flops 5767168 | bytes 25952260 | tf_op jit(solution)/shard_map/jit(_where)/select_n | solution.py:105
  681.9 3.2 broadcast_select_fusion.1
  (205 shorter events, 53.8 us)
Async XLA Ops:
  7.2 541.6 %copy-start = (bf16[2816,512]{1,0:T(8,128)(2,1)S(1)}, bf16[2816,512]{1,0:T(8,128)(2,1)}, u32[]{:S(2)}) copy-start(bf16[2816,512]{1,0:T(8,128)(2,1)} %param.37) | copy-start | bytes 8650756
  9.3 2.3 copy-start.26
  10.8 1.6 copy-start.19
  71.3 6.5 copy-start.10
  71.3 210.8 %copy-start.16 = (f32[2048]{0:T(1024)S(1)}, f32[2048]{0:T(1024)}, u32[]{:S(2)}) copy-start(f32[2048]{0:T(1024)} %param.21) | copy-start | bytes 24580
  71.3 213.0 %copy-start.17 = (s32[32,16]{0,1:T(8,128)S(1)}, s32[32,16]{0,1:T(8,128)}, u32[]{:S(2)}) copy-start(s32[32,16]{0,1:T(8,128)} %param.27) | copy-start | bytes 6148
  71.3 479.3 %all-to-all-start.2 = ((bf16[2,3,8,176,512]{4,3,1,0,2:T(8,128)(2,1)}), bf16[2,3,8,176,512]{4,3,1,0,2:T(8,128)(2,1)}, u32[]{:S(2)}, u32[]{:S(2)}) async-start(bf16[2,3,8,176,512]{4,3,1,0,2:T(8,128)(2,1)} %copy.166), calls=%async_computation.2 | async-start | bytes 17301504 | tf_op jit(solution)/shard_map/all_to_all | solution.py:55
  77.7 327.9 %all-reduce.8.cloned.1.call-start = ((), (), s32[]{:S(2)}) async-start(), calls=%async_computation.4 | async-start | bytes 131072
  284.3 0.6 copy-start.3
  286.8 55.8 %copy-start.1 = (bf16[512,512]{0,1:T(8,128)(2,1)}, bf16[512,512]{0,1:T(8,128)(2,1)S(1)}, u32[]{:S(2)}) copy-start(bf16[512,512]{0,1:T(8,128)(2,1)S(1)} %copy.145) | copy-start | bytes 1572868
  287.8 0.6 copy-start.4
  291.7 2.0 copy-start.23
  292.3 0.6 copy-start.15
  293.6 0.6 copy-start.25
  295.1 0.6 copy-start.7
  295.1 0.6 copy-start.8
  302.9 3.3 copy-start.6
  331.3 0.8 copy-start.2
  332.9 12.5 %copy-start.13 = (f32[8,2]{0,1:T(2,128)}, f32[8,2]{0,1:T(2,128)S(1)}, u32[]{:S(2)}) copy-start(f32[8,2]{0,1:T(2,128)S(1)} %get-tuple-element.98) | copy-start | bytes 196
  333.8 11.6 %copy-start.9 = (f32[4,8,2,1]{1,0,3,2:T(4,128)}, f32[4,8,2,1]{1,0,3,2:T(4,128)S(1)}, u32[]{:S(2)}) copy-start(f32[4,8,2,1]{1,0,3,2:T(4,128)S(1)} %copy.182) | copy-start | bytes 772
  337.6 0.6 copy-start.5
  338.2 10.3 %copy-start.14 = (f32[4,8,2,1]{1,0,3,2:T(4,128)S(1)}, f32[4,8,2,1]{1,0,3,2:T(4,128)}, u32[]{:S(2)}) copy-start(f32[4,8,2,1]{1,0,3,2:T(4,128)} %copy.183) | copy-start | bytes 772
  338.2 14.2 %copy-start.21 = (s32[32,6]{0,1:T(8,128)S(1)}, s32[32,6]{0,1:T(8,128)}, u32[]{:S(2)}) copy-start(s32[32,6]{0,1:T(8,128)} %param.30) | copy-start | bytes 2308
  338.2 14.5 %copy-start.20 = (s32[32]{0:T(128)S(1)}, s32[32]{0:T(128)}, u32[]{:S(2)}) copy-start(s32[32]{0:T(128)} %copy-done.19) | copy-start | bytes 388
  338.2 33.5 %copy-start.22 = (f32[32,6]{0,1:T(8,128)S(1)}, f32[32,6]{0,1:T(8,128)}, u32[]{:S(2)}) copy-start(f32[32,6]{0,1:T(8,128)} %param.31) | copy-start | bytes 2308
  338.2 33.8 %copy-start.28 = (u32[32]{0:T(128)S(1)}, u32[32]{0:T(128)}, u32[]{:S(2)}) copy-start(u32[32]{0:T(128)} %constant.206) | copy-start | bytes 388
  338.3 67.3 %copy-start.11 = (bf16[1,2048]{1,0:T(2,128)(2,1)S(1)}, bf16[1,2048]{1,0:T(2,128)(2,1)}, u32[]{:S(2)}) copy-start(bf16[1,2048]{1,0:T(2,128)(2,1)} %param.20) | copy-start | bytes 12292
  338.3 70.1 %copy-start.18 = (f32[2048]{0:T(1024)S(1)}, f32[2048]{0:T(1024)}, u32[]{:S(2)}) copy-start(f32[2048]{0:T(1024)} %param.29) | copy-start | bytes 24580
  352.4 137.9 %all-reduce.12.cloned.1.call-start = ((), (), s32[]{:S(2)}) async-start(), calls=%async_computation.6 | async-start | bytes 1622016 | tf_op jit(solution)/shard_map/psum | solution.py:275
  442.7 106.1 %all-reduce.10.cloned.1.call-start = ((), (), s32[]{:S(2)}) async-start(), calls=%async_computation.5 | async-start | bytes 131072
  490.3 4.7 copy-start.24
  490.3 58.5 %copy-start.12 = (f32[2,4,2816]{2,1,0:T(4,128)S(1)}, f32[2,4,2816]{2,1,0:T(4,128)}, u32[]{:S(2)}) copy-start(f32[2,4,2816]{2,1,0:T(4,128)} %get-tuple-element.87) | copy-start | bytes 270340
  550.6 16.1 %all-to-all-start.1 = ((f32[4,1,512]{2,1,0:T(1,128)}), f32[4,1,512]{2,1,0:T(1,128)S(1)}, u32[]{:S(2)}, u32[]{:S(2)}) async-start(f32[4,1,512]{2,1,0:T(1,128)} %copy.164), calls=%async_computation.1 | async-start | bytes 16384 | tf_op jit(solution)/shard_map/all_to_all | solution.py:284
  566.7 4.6 copy-start.27
  566.7 101.4 %all-to-all-start.3 = ((bf16[8,3,176,512]{3,2,1,0:T(8,128)(2,1)}), bf16[8,3,176,512]{3,2,1,0:T(8,128)(2,1)}, u32[]{:S(2)}, u32[]{:S(2)}) async-start(bf16[8,3,176,512]{3,2,1,0:T(8,128)(2,1)} %broadcast_select_fusion.2), calls=%async_computation.3 | async-start | bytes 8650752 | tf_op jit(solution)/shard_map/all_to_all | solution.py:103
  670.6 11.3 %slice-start = ((s8[5767168]{0:T(1024)(128)(4,1)}), s8[4194304]{0:T(1024)(128)(4,1)S(1)}, s32[]{:S(2)}) async-start(s8[5767168]{0:T(1024)(128)(4,1)} %bitcast.223), calls=%async_computation.7 | async-start | bytes 8388608
  670.9 11.0 %slice-start.1 = ((s8[5767168]{0:T(1024)(128)(4,1)}), s8[1572864]{0:T(1024)(128)(4,1)S(1)}, s32[]{:S(2)}) async-start(s8[5767168]{0:T(1024)(128)(4,1)} %bitcast.223), calls=%async_computation.8 | async-start | bytes 3145728
Sparse Core Ops, SparseCore 0:
  352.5 53.0 all-reduce.7
  442.8 47.3 all-reduce.11
  495.1 53.6 all-reduce.9

commit v2 on v1

--- a/solution.py
+++ b/solution.py
@@ -48,15 +48,32 @@
     return lax.all_gather(by_expert, "dp", axis=0, tiled=True)
 
 
-def spread_slots(gate_up, down, picks, ex_count):
-    chosen = jnp.concatenate([gate_up[picks], down[picks][:, None]], axis=1)
+def pick_rows(table, rows):
+    return jnp.stack([lax.dynamic_index_in_dim(table, rows[k], 0, False) for k in range(rows.shape[0])])
+
+
+def pick_slots(gate_up, down, picks):
+    return jnp.concatenate([pick_rows(gate_up, picks), pick_rows(down, picks)[:, None]], axis=1)
+
+
+def spread_slots(chosen, ex_count):
     count, parts, ff_width, col_width = chosen.shape
     pieces = chosen.reshape(count, parts, ex_count, ff_width // ex_count, col_width)
     spread = lax.all_to_all(pieces, "expert", split_axis=2, concat_axis=0, tiled=True)
     return spread.reshape(ex_count * count, parts, ff_width // ex_count, col_width)
 
 
-def migrate(expert_gate_up, expert_down, old_place, new_place, ex_index):
+def scatter_sum(values, axis):
+    count = lax.axis_size(axis)
+    received = lax.all_to_all(values, axis, split_axis=0, concat_axis=0, tiled=True)
+    return jnp.sum(received.reshape((count, -1) + values.shape[1:]), axis=0)
+
+
+def sum_over(values, axis):
+    return jnp.sum(lax.all_gather(values, axis, axis=0, tiled=False), axis=0)
+
+
+def migrate_start(expert_gate_up, expert_down, old_place, new_place, ex_index):
     rows, slots_local = old_place.shape
     slots = rows * slots_local
     ex_count = rows
@@ -89,21 +106,29 @@
     src_dev = source // slots_local
     src_rank = rank.reshape(-1)[source]
     fast = min(2, slots_local)
-    spread_a = spread_slots(expert_gate_up, expert_down, my_picks[:fast], ex_count)
-    out_a = spread_a[src_dev * fast + jnp.minimum(src_rank, fast - 1)]
+    chosen = pick_slots(expert_gate_up, expert_down, my_picks[:fast])
+    return chosen, (my_picks, src_dev, src_rank, load, moved_slot[ex_index])
+
+
+def migrate_finish(chosen, plan, expert_gate_up, expert_down):
+    my_picks, src_dev, src_rank, load, my_moved = plan
+    ex_count = src_dev.shape[0]
+    slots_local = expert_gate_up.shape[0]
+    fast = chosen.shape[0]
+    spread_a = spread_slots(chosen, ex_count)
+    out_a = pick_rows(spread_a, src_dev * fast + jnp.minimum(src_rank, fast - 1))
     if slots_local > fast:
         rest = slots_local - fast
 
         def extra():
-            spread_b = spread_slots(expert_gate_up, expert_down, my_picks[fast:], ex_count)
-            return spread_b[src_dev * rest + jnp.clip(src_rank - fast, 0, rest - 1)]
-
-        out_b = lax.cond(load > fast, extra, lambda: jnp.zeros_like(out_a))
-        out_a = jnp.where((src_rank < fast)[:, None, None, None], out_a, out_b)
+            spread_b = spread_slots(pick_slots(expert_gate_up, expert_down, my_picks[fast:]), ex_count)
+            out_b = pick_rows(spread_b, src_dev * rest + jnp.clip(src_rank - fast, 0, rest - 1))
+            return jnp.where((src_rank < fast)[:, None, None, None], out_a, out_b)
+
+        out_a = lax.cond(load > fast, extra, lambda: out_a)
     arrived = lax.all_to_all(out_a, "expert", split_axis=0, concat_axis=2, tiled=True)
-    is_moved = local_ids == moved_slot[ex_index]
-    moved_gate_up = jnp.where(is_moved[:, None, None, None], arrived[:, :2], expert_gate_up)
-    moved_down = jnp.where(is_moved[:, None, None], arrived[:, 2], expert_down)
+    moved_gate_up = lax.dynamic_update_index_in_dim(expert_gate_up, arrived[0, :2], my_moved, 0)
+    moved_down = lax.dynamic_update_index_in_dim(expert_down, arrived[0, 2], my_moved, 0)
     return moved_gate_up, moved_down
 
 
@@ -137,7 +162,9 @@
     head_local = query_weight.shape[0] // (NOPE + ROPE)
     score_scale = (NOPE + ROPE) ** (-0.5)
     group_start = dp_index * group_rows
+    chosen, plan = migrate_start(expert_gate_up, expert_down, old_place, new_place, ex_index)
     everyone = gather_rows(hidden)
+    everyone, chosen = lax.optimization_barrier((everyone, chosen))
     normed = rms_norm(everyone.astype(jnp.float32), attn_gain).astype(jnp.bfloat16)
     queries = jnp.einsum(
         "td,qd->tq", normed, query_weight, preferred_element_type=jnp.float32
@@ -223,7 +250,7 @@
     )
     heads_out = heads_out.astype(jnp.bfloat16).reshape(group_rows, head_local * VHEAD)
     partial_value = jnp.dot(heads_out, out_weight, preferred_element_type=jnp.float32)
-    attn_out = lax.psum_scatter(partial_value, "expert", scatter_dimension=0, tiled=True)
+    attn_out = scatter_sum(partial_value, "expert")
     residual = hidden.astype(jnp.float32) + attn_out
     normed_ffn = rms_norm(residual, ffn_gain).astype(jnp.bfloat16)
     slots_local = expert_gate_up.shape[0]
@@ -272,7 +299,7 @@
     shared_part = jnp.einsum(
         "td,gfd->gtf", column_rows, shared_gate_up, preferred_element_type=jnp.float32
     )
-    routed_sum, shared_sum = lax.psum((routed_part, shared_part), "dp")
+    routed_sum, shared_sum = sum_over(routed_part, "dp"), sum_over(shared_part, "dp")
     activated = (jax.nn.silu(routed_sum[:, 0]) * routed_sum[:, 1]).astype(jnp.bfloat16)
     slot_out = jnp.einsum(
         "scf,sfd->scd", activated, expert_down, preferred_element_type=jnp.float32
@@ -280,10 +307,10 @@
     routed = jnp.einsum("tsc,scd->td", combine, slot_out, precision=HIGHEST)
     shared_act = (jax.nn.silu(shared_sum[0]) * shared_sum[1]).astype(jnp.bfloat16)
     shared_term = jnp.dot(shared_act, shared_down, preferred_element_type=jnp.float32)
-    moe_rows = lax.psum_scatter(routed, "expert", scatter_dimension=0, tiled=True)
+    moe_rows = scatter_sum(routed, "expert")
     moe_part = lax.all_to_all(moe_rows + shared_term, "dp", split_axis=0, concat_axis=1, tiled=True)
     layer_out = (residual + moe_part).astype(jnp.bfloat16)
-    moved_gate_up, moved_down = migrate(expert_gate_up, expert_down, old_place, new_place, ex_index)
+    moved_gate_up, moved_down = migrate_finish(chosen, plan, expert_gate_up, expert_down)
     return (layer_out, moved_gate_up, moved_down)
 
 

time: 694 us -> 567 us (0.82)
  blocking collectives: 238 us -> 74.1 us
  waiting for transfers between devices: 228 us -> 293 us
  other arithmetic: 79.7 us -> 43.5 us
  between operations: 18.1 us -> 38.7 us
  local copies, waits for them, and re-layouts: 79.7 us -> 68.9 us
    all_gather x2, blocking collectives: 210 us -> 30.3 us  [gather_rows(): by_expert = lax.all_gather(rows, 'expert', axis=0, tiled=True)]
    all_to_all x1, waiting for transfers between devices: 0.01 us -> 157 us  [spread_slots(): lax.all_to_all(pieces, 'expert', split_axis=2, concat_axis=0, tiled=True)]
    unnamed x5 -> x1, waiting for transfers between devices: 86.1 us -> 0.02 us
    psum x1 -> x0, waiting for transfers between devices: 46.9 us -> none  [local(): routed_sum, shared_sum = lax.psum((routed_part, shared_part), 'dp')]
    all_gather x0 -> x1, waiting for transfers between devices: none -> 42.1 us  [sum_over(): return jnp.sum(lax.all_gather(values, axis, axis=0, tiled=False), axis=0)]
    gather x8 -> x2, local copies, waits for them, and re-layouts: 34.7 us -> 1.3 us  [the longest x1 0.65 us: migrate_start(): wanted = jnp.take_along_axis(new_place, moved_slot[:, None], axis=1)[:, 0]]
    unnamed x73, local copies, waits for them, and re-layouts: 10.5 us -> 33.3 us
    select_n x8 -> x3, other arithmetic: 21.5 us -> 0.02 us  [the longest x1 0.01 us: migrate_start(): wanted = jnp.take_along_axis(new_place, moved_slot[:, None], axis=1)[:, 0]]
  transfers between devices with their start and end apart: 6 -> 5, of which waited for: 4 -> 3; matrix products, arithmetic and copies ran while one was open for 16% -> 6% of each run, Pallas kernels for 0% -> 0%
where the time goes in v2:
time: 567 us; the launch traced here: 565 us
  waiting for transfers between devices  293 us (52%)
  blocking collectives  74.1 us (13%)
  local copies, waits for them, and re-layouts  68.9 us (12%)
  other arithmetic  43.5 us (8%)
  between operations  38.7 us (7%)
  matrix products  27.7 us (5%)
  starting transfers between devices  19.2 us (3%)
    all_to_all x1, waiting for transfers between devices, spread_slots(): lax.all_to_all(pieces, 'expert', split_axis=2, concat_axis=0, tiled=True)  157 us
    all_to_all x1, waiting for transfers between devices, migrate_finish(): lax.all_to_all(out_a, 'expert', split_axis=0, concat_axis=2, tiled=True)  93.7 us
    all_gather x1, waiting for transfers between devices, sum_over(): return jnp.sum(lax.all_gather(values, axis, axis=0, tiled=False), axis=0)  42.1 us
    unnamed x73, local copies, waits for them, and re-layouts  33.3 us
    all_gather x2, blocking collectives, gather_rows(): by_expert = lax.all_gather(rows, 'expert', axis=0, tiled=True)  30.3 us
    all_gather x2, blocking collectives, gather_rows(): return lax.all_gather(by_expert, 'dp', axis=0, tiled=True)  15.8 us
    all_gather x1, blocking collectives, local(): gathered = lax.all_gather(packed, 'dp', axis=0, tiled=False)  11.4 us
  transfers between devices with their start and end apart: 5, of which 3 were waited for; matrix products, arithmetic and copies ran while one was open for 6% of the time, Pallas kernels for 0%

profile of v2, /device:TPU:0, one launch (start us, length us, event | category | flops | bytes accessed | tf_op | source)
XLA Modules:
  0.0 565.2 jit_solution(12884834417249530408)
XLA Ops:
  7.2 6.1 %copy.256 = bf16[4,1408,512]{2,1,0:T(8,128)(2,1)} copy(bf16[4,1408,512]{2,1,0:T(8,128)(2,1)} %param.35) | data formatting | bytes 11534336
  13.3 2.1 copy-done.4
  15.4 4.4 copy.255
  33.6 2.4 scatter_custom_fusion
  37.2 1.3 copy.162
  38.5 15.7 %all-gather.3 = bf16[8,1,2048]{2,1,0:T(2,128)(2,1)S(1)} all-gather(bf16[1,1,2048]{2,1,0:T(2,128)(2,1)S(1)} %bitcast.260), channel_id=1, replica_groups=mesh['dp'=4,'expert'=8] {'expert'}, dimensions={0}, use_global_device_ids=true | all-gather | bytes 36864 | tf_op jit(solution)/shard_map/all_gather | solution.py:47
  54.2 8.5 %all_gather.31 = bf16[32,2048]{1,0:T(8,128)(2,1)S(1)} all-gather(bf16[8,2048]{1,0:T(8,128)(2,1)S(1)} %bitcast.257), channel_id=1, replica_groups=mesh['dp'=4,'expert'=8] {'dp'}, dimensions={0}, use_global_device_ids=true | all-gather | bytes 163840 | tf_op jit(solution)/shard_map/all_gather | solution.py:48
  63.9 2.0 constant_dynamic-slice_fusion.9
  65.9 3.1 constant_dynamic-slice_fusion.11
  69.3 3.8 pad_maximum_fusion.3
  79.8 1.6 fusion.6
  81.4 1.3 fusion.90
  85.3 1.5 convolution_multiply_fusion
  88.8 11.4 %all-gather = f32[128,2,514]{2,0,1:T(8,128)S(1)} all-gather(f32[32,2,514]{2,0,1:T(8,128)S(1)} %pad_maximum_fusion.4), channel_id=2, replica_groups=mesh['dp'=4,'expert'=8] {'dp'}, dimensions={0}, use_global_device_ids=true | all-gather | bytes 657920 | tf_op jit(solution)/shard_map/all_gather | solution.py:220
  100.8 2.6 copy.204
  105.0 3.0 multiply_reduce_fusion
  109.1 2.4 fusion.24
  113.1 1.8 convolution_bitcast_fusion.2
  115.5 4.7 all-to-all-start.1
  120.3 1.3 iota_reduce_fusion
  124.0 4.5 compare_select_fusion.3
  128.6 10.4 %select_subtract_fusion = s32[192]{0:T(256)S(1)} fusion(pred[192]{0:T(512)(128)(4,1)S(1)} %get-tuple-element.100, pred[192]{0:T(512)(128)(4,1)S(1)} %get-tuple-element.99, pred[192]{0:T(512)(128)(4,1)S(1)} %get-tuple-element.98, pred[192]{0:T(512)(128)(4,1)S(1)} %get-tuple-element.97, pred[192]{0:T(512)(128)(4,1)S(1)} %get-tuple-element.96, ...), kind=kLoop, calls=%fused_computation.220 | loop fusion | flops 3456 | bytes 4872 | tf_op jit(solution)/shard_map/sub | solution.py:283
  139.1 1.2 reduce-window.6
  143.4 14.6 %all-gather.4 = bf16[8,1,2048]{2,1,0:T(2,128)(2,1)S(1)} all-gather(bf16[1,1,2048]{2,1,0:T(2,128)(2,1)S(1)} %convert_bitcast_fusion), channel_id=1, replica_groups=mesh['dp'=4,'expert'=8] {'expert'}, dimensions={0}, use_global_device_ids=true | all-gather | bytes 36864 | tf_op jit(solution)/shard_map/all_gather | solution.py:47
  158.0 7.3 %all_gather.35 = bf16[32,2048]{1,0:T(8,128)(2,1)S(1)} all-gather(bf16[8,2048]{1,0:T(8,128)(2,1)S(1)} %bitcast.258), channel_id=1, replica_groups=mesh['dp'=4,'expert'=8] {'dp'}, dimensions={0}, use_global_device_ids=true | all-gather | bytes 163840 | tf_op jit(solution)/shard_map/all_gather | solution.py:48
  165.4 6.9 %convolution_bitcast_fusion.1 = f32[4,2,16,1408]{3,2,1,0:T(8,128)} fusion(bf16[4,2,1408,512]{3,2,1,0:T(8,128)(2,1)} %copy.255, bf16[32,512,1]{1,0,2:T(8,128)(2,1)S(1)} %reshape.541, bf16[32,4,16]{0,2,1:T(8,128)(2,1)S(1)} %get-tuple-element.82), kind=kOutput, calls=%fused_computation.28 | convolution fusion | flops 186679296 | bytes 12292096 | tf_op jit(solution)/shard_map/scd,sgfd->sgcf/dot_general | solution.py:296
  172.3 42.1 %all-gather.7.cloned.1.call-done = f32[16,2,16,1408]{3,2,1,0:T(8,128)} async-done(((f32[4,2,16,1408]{3,2,1,0:T(8,128)}), f32[16,2,16,1408]{3,2,1,0:T(8,128)}) %all-gather.7.cloned.1.call-update) | async-done | bytes 2883600 | tf_op jit(solution)/shard_map/all_gather | solution.py:73
  214.4 2.9 reduce_sum.140
  217.3 3.7 convolution_bitcast_fusion.3
  222.1 4.6 all-to-all-start.2
  226.7 7.6 %copy.185 = bf16[2,3,8,176,512]{4,3,1,0,2:T(8,128)(2,1)} copy(bf16[2,3,8,176,512]{4,3,2,1,0:T(8,128)(2,1)} %bitcast.244) | data formatting | bytes 17301504 | tf_op jit(solution)/shard_map/reshape | solution.py:61
  234.2 5.1 all-to-all-start.4
  257.3 4.2 convolution_bitcast_fusion
  261.5 9.5 %all-gather.2 = f32[8,4,2816]{2,1,0:T(4,128)S(1)} all-gather(f32[2,4,2816]{2,1,0:T(4,128)S(1)} %convolution_bitcast_fusion), channel_id=4, replica_groups=mesh['dp'=4,'expert'=8] {'dp'}, dimensions={0}, use_global_device_ids=true | all-gather | bytes 450560 | tf_op jit(solution)/shard_map/all_gather | solution.py:73
  271.6 157.4 %all-to-all-done.4 = bf16[2,3,8,176,512]{4,3,1,0,2:T(8,128)(2,1)} async-done(((bf16[2,3,8,176,512]{4,3,1,0,2:T(8,128)(2,1)}), bf16[2,3,8,176,512]{4,3,1,0,2:T(8,128)(2,1)}, u32[]{:S(2)}, u32[]{:S(2)}) %all-to-all-start.4) | async-done | bytes 8650784 | tf_op jit(solution)/shard_map/all_to_all | solution.py:62
  429.0 1.9 dynamic-slice_dynamic-update-slice_fusion.15
  430.9 1.9 dynamic-slice_dynamic-update-slice_fusion.14
  432.8 1.9 dynamic-slice_dynamic-update-slice_fusion.13
  434.7 1.9 dynamic-slice_dynamic-update-slice_fusion.12
  436.5 1.9 dynamic-slice_dynamic-update-slice_fusion.11
  438.5 1.9 dynamic-slice_dynamic-update-slice_fusion.10
  440.3 1.9 dynamic-slice_dynamic-update-slice_fusion.9
  442.2 1.9 dynamic-slice_dynamic-update-slice_fusion.8
  444.1 7.2 %all_to_all.76 = f32[4,1,512]{2,1,0:T(1,128)S(1)} all-to-all(f32[4,1,512]{2,1,0:T(1,128)S(1)} %copy.184), channel_id=1, replica_groups=mesh['dp'=4,'expert'=8] {'dp'}, dimensions={0} | all-to-all | bytes 16384 | tf_op jit(solution)/shard_map/all_to_all | solution.py:311
  451.3 4.7 all-to-all-start.5
  459.2 93.7 %all-to-all-done.5 = bf16[8,3,176,512]{3,2,1,0:T(8,128)(2,1)} async-done(((bf16[8,3,176,512]{3,2,1,0:T(8,128)(2,1)}), bf16[8,3,176,512]{3,2,1,0:T(8,128)(2,1)}, u32[]{:S(2)}, u32[]{:S(2)}) %all-to-all-start.5) | async-done | bytes 4325408 | tf_op jit(solution)/shard_map/all_to_all | solution.py:129
  552.8 2.5 copy.187
  555.3 1.8 slice_dynamic-update-slice_fusion
  (197 shorter events, 38.6 us)
Async XLA Ops:
  7.2 263.9 %copy-start = (bf16[2816,512]{1,0:T(8,128)(2,1)S(1)}, bf16[2816,512]{1,0:T(8,128)(2,1)}, u32[]{:S(2)}) copy-start(bf16[2816,512]{1,0:T(8,128)(2,1)} %param.37) | copy-start | bytes 8650756
  7.2 8.2 %copy-start.4 = (bf16[4,2,1408,512]{3,2,1,0:T(8,128)(2,1)S(1)}, bf16[4,2,1408,512]{3,2,1,0:T(8,128)(2,1)}, u32[]{:S(2)}) copy-start(bf16[4,2,1408,512]{3,2,1,0:T(8,128)(2,1)} %param.34) | copy-start | bytes 34603012
  15.4 4.4 copy-start.19
  15.4 4.6 copy-start.2
  15.4 17.9 %copy-start.17 = (s32[32,16]{0,1:T(8,128)S(1)}, s32[32,16]{0,1:T(8,128)}, u32[]{:S(2)}) copy-start(s32[32,16]{0,1:T(8,128)} %param.27) | copy-start | bytes 6148
  15.4 23.1 %copy-start.8 = (bf16[1,2048]{1,0:T(2,128)(2,1)S(1)}, bf16[1,2048]{1,0:T(2,128)(2,1)}, u32[]{:S(2)}) copy-start(bf16[1,2048]{1,0:T(2,128)(2,1)} %param.20) | copy-start | bytes 12292
  20.0 12.7 %copy-start.23 = (s32[32]{0:T(128)}, s32[32]{0:T(128)S(1)}, u32[]{:S(2)}) copy-start(s32[32]{0:T(128)S(1)} %eq.142) | copy-start | bytes 388
  20.5 6.5 %copy-start.26 = (s32[8]{0:T(128)}, s32[8]{0:T(128)S(1)}, u32[]{:S(2)}) copy-start(s32[8]{0:T(128)S(1)} %get-tuple-element.36) | copy-start | bytes 100
  22.0 0.8 copy-start.21
  22.7 0.5 copy-start.24
  29.0 0.6 copy-start.14
  36.7 0.5 copy-start.16
  38.5 36.3 %copy-start.5 = (bf16[512,512]{0,1:T(8,128)(2,1)}, bf16[512,512]{0,1:T(8,128)(2,1)S(1)}, u32[]{:S(2)}) copy-start(bf16[512,512]{0,1:T(8,128)(2,1)S(1)} %copy.162) | copy-start | bytes 1572868
  69.3 4.0 copy-start.18
  69.3 4.7 copy-start.6
  73.4 0.6 copy-start.7
  79.1 0.7 copy-start.9
  79.1 4.7 copy-start.11
  104.0 8.4 %copy-start.10 = (bf16[32,2,32]{2,1,0:T(2,128)(2,1)S(1)}, bf16[32,2,32]{2,1,0:T(2,128)(2,1)}, u32[]{:S(2)}) copy-start(bf16[32,2,32]{2,1,0:T(2,128)(2,1)} %copy-done.9) | copy-start | bytes 12292
  104.0 8.4 %copy-start.12 = (bf16[32,2,32]{2,1,0:T(2,128)(2,1)S(1)}, bf16[32,2,32]{2,1,0:T(2,128)(2,1)}, u32[]{:S(2)}) copy-start(bf16[32,2,32]{2,1,0:T(2,128)(2,1)} %copy-done.11) | copy-start | bytes 12292
  104.0 8.8 %copy-start.13 = (bf16[8,2,512]{2,0,1:T(8,128)(2,1)S(1)}, bf16[8,2,512]{2,0,1:T(8,128)(2,1)}, u32[]{:S(2)}) copy-start(bf16[8,2,512]{2,0,1:T(8,128)(2,1)} %dynamic-slice_bitcast_fusion.2) | copy-start | bytes 49156
  104.0 39.3 %copy-start.20 = (f32[2048]{0:T(1024)S(1)}, f32[2048]{0:T(1024)}, u32[]{:S(2)}) copy-start(f32[2048]{0:T(1024)} %param.29) | copy-start | bytes 24580
  115.5 26.4 %all-to-all-start.1 = ((f32[8,1,2048]{2,1,0:T(1,128)}), f32[8,1,2048]{2,1,0:T(1,128)S(1)}, u32[]{:S(2)}, u32[]{:S(2)}) async-start(f32[8,1,2048]{2,1,0:T(1,128)} %copy.173), calls=%async_computation.1 | async-start | bytes 131072 | tf_op jit(solution)/shard_map/all_to_all | solution.py:68
  120.3 94.2 %all-gather.7.cloned.1.call-start = ((), (), s32[]{:S(2)}) async-start(), calls=%async_computation.6 | async-start | bytes 3604480 | tf_op jit(solution)/shard_map/all_gather | solution.py:73
  222.1 12.2 %all-to-all-start.2 = ((f32[8,4,512]{2,1,0:T(4,128)}), f32[8,4,512]{2,1,0:T(4,128)S(1)}, u32[]{:S(2)}, u32[]{:S(2)}) async-start(f32[8,4,512]{2,1,0:T(4,128)} %convolution_bitcast_fusion.4), calls=%async_computation.2 | async-start | bytes 131072 | tf_op jit(solution)/shard_map/all_to_all | solution.py:68
  234.2 6.5 %copy-start.22 = (s32[8]{0:T(128)S(1)}, s32[8]{0:T(128)}, u32[]{:S(2)}) copy-start(s32[8]{0:T(128)} %copy-done.21) | copy-start | bytes 100
  234.2 6.5 %copy-start.25 = (s32[8]{0:T(128)S(1)}, s32[8]{0:T(128)}, u32[]{:S(2)}) copy-start(s32[8]{0:T(128)} %copy-done.24) | copy-start | bytes 100
  234.2 194.7 %all-to-all-start.4 = ((bf16[2,3,8,176,512]{4,3,1,0,2:T(8,128)(2,1)}), bf16[2,3,8,176,512]{4,3,1,0,2:T(8,128)(2,1)}, u32[]{:S(2)}, u32[]{:S(2)}) async-start(bf16[2,3,8,176,512]{4,3,1,0,2:T(8,128)(2,1)} %copy.185), calls=%async_computation.4 | async-start | bytes 17301504 | tf_op jit(solution)/shard_map/all_to_all | solution.py:62
  429.0 15.1 %copy-start.15 = (s32[1,4]{0,1:T(4,128)S(1)}, s32[1,4]{0,1:T(4,128)}, u32[]{:S(2)}) copy-start(s32[1,4]{0,1:T(4,128)} %copy-done.14) | copy-start | bytes 52
  451.3 4.7 copy-start.27
  451.3 101.5 %all-to-all-start.5 = ((bf16[8,3,176,512]{3,2,1,0:T(8,128)(2,1)}), bf16[8,3,176,512]{3,2,1,0:T(8,128)(2,1)}, u32[]{:S(2)}, u32[]{:S(2)}) async-start(bf16[8,3,176,512]{3,2,1,0:T(8,128)(2,1)} %get-tuple-element.179), calls=%async_computation.5 | async-start | bytes 8650752 | tf_op jit(solution)/shard_map/all_to_all | solution.py:129
  555.3 3.0 copy-start.1
Sparse Core Ops, SparseCore 0:
  172.4 41.9 all-gather.6
